TPU v7x, 256 devices: a whole 4x4x8 slice. The times are simulated.
256 devices in a mesh: req: 8 (over x, z_hi), blk: 32 (over y, z_lo, core).
Axes of the slice: x: 4, y: 4, z: 8 (z_hi: 2, z_lo: 4; z = z_hi * 4 + z_lo), core: 2. Of those that a mesh axis runs over, the one named last changes fastest.
Arguments:
- tokens: bfloat16 [256, 128, 1536], P(('req', 'blk')), may hold values from -6 to 6
- cache_kv: bfloat16 [256, 2, 256, 384], P(('req', 'blk')), may hold values from -200 to 200
- cache_len: int32 [256], P(('req', 'blk')), may hold values from 2 to 256, as said below
- holder: int32 [256], P(('req', 'blk')), may hold values from 0 to 7, as said below
- accept: int32 [256, 128], P(('req', 'blk')), may hold values from 0 to 1, as said below
- attn_gain: float32 [1536], replicated, may hold values from 0.1 to 1.9
- q_weight: bfloat16 [1536, 768], replicated, may hold values from -0.15625 to 0.15625
- k_weight: bfloat16 [1536, 384], replicated, may hold values from -0.15625 to 0.15625
- v_weight: bfloat16 [1536, 384], replicated, may hold values from -0.15625 to 0.15625
- o_weight: bfloat16 [768, 1536], replicated, may hold values from -0.21875 to 0.21875
- ffn_gain: float32 [1536], replicated, may hold values from 0.4 to 2.5
- w_gate: bfloat16 [1536, 4096], P(None, 'blk'), may hold values from -0.15625 to 0.15625
- w_up: bfloat16 [1536, 4096], P(None, 'blk'), may hold values from -0.15625 to 0.15625
- w_down: bfloat16 [4096, 1536], P('blk'), may hold values from -0.09375 to 0.09375
Outputs:
- refined: float32 [256, 128, 1536], P(('req', 'blk'))
Inputs may be any that keep to these rules, and one draw needn't show every extreme that they name: `holder`: requests whose numbers agree modulo 32 have distinct holders. `cache_len`: some request has exactly 256 cached positions. `accept`: each request accepts exactly 64 positions.
All inputs are finite; a program needn't handle non-finite values.
Results may differ from a plain program's by a relative error of at most 0.04.
Values may be sent and summed in bfloat16 or wider, within the bound.
No kernel may reach another device: no remote copies, remote signals or barrier semaphores. Data moves between devices by JAX's collectives and lax.ppermute only.
A program may use at most 128 MiB of HBM per device.

v0:
```python
import jax
import jax.numpy as jnp
from jax import lax
from jax.sharding import PartitionSpec as P

HEAD = 96
norm_eps = 1e-05
rope_base = 100000.0


def rms_scale(values, gain_row):
    return (
        values * lax.rsqrt(jnp.mean(values * values, axis=-1, keepdims=True) + norm_eps) * gain_row
    )


def rotate_heads(flat, positions, head_count):
    half_dim = HEAD // 2
    shaped = flat.reshape(flat.shape[0], head_count, HEAD)
    freqs = jnp.exp(-jnp.log(rope_base) * 2.0 * jnp.arange(half_dim, dtype=jnp.float32) / HEAD)
    angles = positions[:, None] * freqs[None, :]
    cosine = jnp.cos(angles)[:, None, :]
    sine = jnp.sin(angles)[:, None, :]
    first_half = shaped[..., :half_dim]
    second_half = shaped[..., half_dim:]
    turned = jnp.concatenate(
        [first_half * cosine - second_half * sine, second_half * cosine + first_half * sine],
        axis=-1,
    )
    return turned.reshape(flat.shape[0], head_count * HEAD)


def attend_block(
    tok_rows,
    cache_keys,
    cache_vals,
    cache_length,
    attn_gain,
    q_weight,
    k_weight,
    v_weight,
    o_weight,
):
    block_len = tok_rows.shape[0]
    slot_len = cache_keys.shape[0]
    kv_count = k_weight.shape[1] // HEAD
    q_count = q_weight.shape[1] // HEAD
    widened = tok_rows.astype(jnp.float32)
    normed = rms_scale(widened, attn_gain).astype(jnp.bfloat16)
    positions = (cache_length + jnp.arange(block_len, dtype=jnp.int32)).astype(jnp.float32)
    queries = rotate_heads(
        jnp.dot(normed, q_weight, preferred_element_type=jnp.float32), positions, q_count
    ).astype(jnp.bfloat16)
    new_keys = rotate_heads(
        jnp.dot(normed, k_weight, preferred_element_type=jnp.float32), positions, kv_count
    ).astype(jnp.bfloat16)
    new_vals = jnp.dot(normed, v_weight, preferred_element_type=jnp.float32).astype(jnp.bfloat16)
    all_keys = jnp.concatenate([cache_keys, new_keys], axis=0).reshape(
        slot_len + block_len, kv_count, HEAD
    )
    all_vals = jnp.concatenate([cache_vals, new_vals], axis=0).reshape(
        slot_len + block_len, kv_count, HEAD
    )
    grouped = queries.reshape(block_len, kv_count, q_count // kv_count, HEAD)
    scores = jnp.einsum(
        "bgid,kgd->gibk", grouped, all_keys, preferred_element_type=jnp.float32
    ) * HEAD ** (-0.5)
    valid = jnp.concatenate(
        [
            jnp.arange(slot_len, dtype=jnp.int32) < cache_length,
            jnp.ones((block_len,), dtype=jnp.bool_),
        ]
    )
    scores = jnp.where(valid, scores, -jnp.inf)
    peaks = jnp.max(scores, axis=-1, keepdims=True)
    expd = jnp.exp(scores - peaks)
    probs = (expd / jnp.sum(expd, axis=-1, keepdims=True)).astype(jnp.bfloat16)
    context = jnp.einsum("gibk,kgd->bgid", probs, all_vals, preferred_element_type=jnp.float32)
    context = context.astype(jnp.bfloat16).reshape(block_len, q_count * HEAD)
    return widened + jnp.dot(context, o_weight, preferred_element_type=jnp.float32)


def run_ffn(normed_rows, w_gate, w_up, w_down, down_all):
    part_rows = lax.all_gather(normed_rows, "blk", axis=0, tiled=True)
    gate_vals = jnp.dot(part_rows, w_gate, preferred_element_type=jnp.float32)
    up_vals = jnp.dot(part_rows, w_up, preferred_element_type=jnp.float32)
    hidden_all = (jax.nn.silu(gate_vals) * up_vals).astype(jnp.bfloat16)
    hidden_own = lax.all_to_all(hidden_all, "blk", 0, 1, tiled=True)
    groups = w_down.shape[0]
    group_count = down_all.shape[0] // groups
    terms = jnp.einsum(
        "rgk,gkd->grd",
        hidden_own.reshape(hidden_own.shape[0], group_count, groups),
        down_all.reshape(group_count, groups, down_all.shape[1]),
        preferred_element_type=jnp.float32,
    ).astype(jnp.bfloat16)
    return jnp.sum(terms.astype(jnp.float32), axis=0)


def fetch_slot(cache_kv, holder):
    count = lax.axis_size("req")
    own = cache_kv[0]
    if count != 8:
        slots = lax.all_gather(own, "req", axis=0, tiled=False)
        return slots[holder[0]]
    me = lax.axis_index("req")

    def swap(values, mask):
        return lax.ppermute(values, "req", perm=[(i, i ^ mask) for i in range(count)])

    def pick(cond, a, b):
        return jnp.where(cond, a, b)

    near = swap(holder, 1)
    quad = swap(jnp.concatenate([holder, near]), 2)
    holders = {0: holder[0], 1: near[0], 2: quad[0], 3: quad[1]}
    got1 = swap(own, 4)
    send_a = pick(holders[2] == me ^ 4, got1, own)
    send_b = pick(holders[3] == me ^ 4, got1, own)
    got2 = swap(jnp.stack([send_a, send_b]), 2)
    want = holders[1]
    send_c = pick(want == me, own, pick(want == me ^ 4, got1, got2[1]))
    got3 = swap(send_c, 1)
    need = holders[0]
    return pick(
        need == me,
        own,
        pick(
            need == me ^ 4, got1, pick(need ^ me == 2, got2[0], pick(need ^ me == 6, got2[0], got3))
        ),
    )


def local(
    tokens,
    cache_kv,
    cache_len,
    holder,
    accept,
    attn_gain,
    q_weight,
    k_weight,
    v_weight,
    o_weight,
    ffn_gain,
    w_gate,
    w_up,
    w_down,
):
    fetched = fetch_slot(cache_kv, holder)
    copies = jnp.broadcast_to(w_down[None], (lax.axis_size("blk"),) + w_down.shape)
    down_all = lax.all_to_all(copies, "blk", 0, 0, tiled=True).reshape(-1, w_down.shape[1])
    fetched, down_all = lax.optimization_barrier((fetched, down_all))
    cache_keys = fetched[0]
    cache_vals = fetched[1]
    cache_length = cache_len[0]
    block_rows = tokens[0]
    first_pass = attend_block(
        block_rows,
        cache_keys,
        cache_vals,
        cache_length,
        attn_gain,
        q_weight,
        k_weight,
        v_weight,
        o_weight,
    )
    chosen_mask = accept[0] == 1
    ffn_sum = run_ffn(
        rms_scale(first_pass, ffn_gain).astype(jnp.bfloat16), w_gate, w_up, w_down, down_all
    )
    placed = first_pass + ffn_sum
    second_in = jnp.where(chosen_mask[:, None], placed, block_rows.astype(jnp.float32))
    refined = attend_block(
        second_in,
        cache_keys,
        cache_vals,
        cache_length,
        attn_gain,
        q_weight,
        k_weight,
        v_weight,
        o_weight,
    )
    return refined[None]


def solution(mesh):
    return jax.shard_map(
        local,
        mesh=mesh,
        in_specs=(
            P(("req", "blk"), None, None),
            P(("req", "blk"), None, None, None),
            P(("req", "blk")),
            P(("req", "blk")),
            P(("req", "blk"), None),
            P(),
            P(),
            P(),
            P(),
            P(),
            P(),
            P(None, "blk"),
            P(None, "blk"),
            P("blk", None),
        ),
        out_specs=P(("req", "blk"), None, None),
        check_vma=False,
    )
```

profile of v0, /device:TPU:1, one launch (start us, length us, event | category | flops | bytes accessed | tf_op | source)
XLA Modules:
  0.0 477.4 jit_solution(10398602093591844268)
XLA Ops:
  6.5 7.1 %broadcast_in_dim.20 = bf16[32,128,1536]{2,1,0:T(8,128)(2,1)} broadcast(bf16[128,1536]{1,0:T(8,128)(2,1)} %param.27), dimensions={1,2} | broadcast | bytes 12976128 | tf_op jit(solution)/shard_map/broadcast_in_dim | solution.py:151
  13.6 10.4 %all-to-all-start = ((bf16[32,128,1536]{2,1,0:T(8,128)(2,1)}), bf16[32,128,1536]{2,1,0:T(8,128)(2,1)}, u32[]{:S(2)}, u32[]{:S(2)}) async-start(bf16[32,128,1536]{2,1,0:T(8,128)(2,1)} %broadcast_in_dim.20), calls=%async_computation | async-start | bytes 25165824 | tf_op jit(solution)/shard_map/all_to_all | solution.py:152
  24.0 2.8 collective-permute-start
  26.9 4.2 collective-permute-start.1
  31.8 4.4 copy.29
  37.0 3.3 fusion.55
  40.8 200.4 %collective-permute-done.1 = s32[1]{0:T(128)} collective-permute-done((s32[1]{0:T(128)}, s32[1]{0:T(128)}, u32[]{:S(2)}, u32[]{:S(2)}) %collective-permute-start.1) | collective-permute-done | bytes 36 | tf_op jit(solution)/shard_map/ppermute | solution.py:109
  249.8 2.5 copy.28
  252.3 1.9 subtract_convert_fusion.1
  254.1 2.3 convolution_convert_fusion.4
  259.0 6.3 %collective-permute-done.3 = bf16[2,2,256,384]{3,2,1,0:T(8,128)(2,1)} collective-permute-done((bf16[2,2,256,384]{3,2,1,0:T(8,128)(2,1)}, bf16[2,2,256,384]{3,2,1,0:T(8,128)(2,1)}, u32[]{:S(2)}, u32[]{:S(2)}) %collective-permute-start.3) | collective-permute-done | bytes 786464 | tf_op jit(solution)/shard_map/ppermute | solution.py:109
  265.3 1.8 fusion.28
  273.1 6.1 %collective-permute-done.4 = bf16[2,256,384]{2,1,0:T(8,128)(2,1)} collective-permute-done((bf16[2,256,384]{2,1,0:T(8,128)(2,1)}, bf16[2,256,384]{2,1,0:T(8,128)(2,1)}, u32[]{:S(2)}, u32[]{:S(2)}) %collective-permute-start.4) | collective-permute-done | bytes 393248 | tf_op jit(solution)/shard_map/ppermute | solution.py:109
  279.2 1.9 fusion.24
  281.1 34.0 %all-to-all-done = bf16[32,128,1536]{2,1,0:T(8,128)(2,1)} async-done(((bf16[32,128,1536]{2,1,0:T(8,128)(2,1)}), bf16[32,128,1536]{2,1,0:T(8,128)(2,1)}, u32[]{:S(2)}, u32[]{:S(2)}) %all-to-all-start) | async-done | bytes 12582944 | tf_op jit(solution)/shard_map/all_to_all | solution.py:152
  316.6 2.8 fusion.78
  319.4 1.7 convolution_convert_fusion.2
  323.6 78.8 %all-gather.2.cloned.1.call-done = bf16[4096,1536]{1,0:T(8,128)(2,1)} async-done(((bf16[128,1536]{1,0:T(8,128)(2,1)}), bf16[4096,1536]{1,0:T(8,128)(2,1)}) %all-gather.2.cloned.1.call-update) | async-done | bytes 12582928 | tf_op jit(solution)/shard_map/all_gather | solution.py:84
  402.4 8.0 %fusion.84 = f32[4096,128]{1,0:T(8,128)S(1)} fusion(bf16[4096,1536]{1,0:T(8,128)(2,1)} %all-gather.2.cloned.1.call-done, bf16[1536,128]{1,0:T(8,128)(2,1)S(1)} %copy-done.12), kind=kOutput, calls=%fused_computation.105 | convolution fusion | flops 1610612736 | bytes 15073280 | tf_op jit(solution)/shard_map/dot_general | solution.py:85
  410.6 4.6 fusion.2
  415.2 6.9 %all-to-all-start.1 = ((bf16[32,128,128]{2,1,0:T(8,128)(2,1)}), bf16[32,128,128]{2,1,0:T(8,128)(2,1)}, u32[]{:S(2)}, u32[]{:S(2)}) async-start(bf16[32,128,128]{2,1,0:T(8,128)(2,1)} %bitcast.158), calls=%async_computation.1 | async-start | bytes 2097152 | tf_op jit(solution)/shard_map/all_to_all | solution.py:88
  422.1 27.9 %all-to-all-done.1 = bf16[32,128,128]{2,1,0:T(8,128)(2,1)} async-done(((bf16[32,128,128]{2,1,0:T(8,128)(2,1)}), bf16[32,128,128]{2,1,0:T(8,128)(2,1)}, u32[]{:S(2)}, u32[]{:S(2)}) %all-to-all-start.1) | async-done | bytes 1048608 | tf_op jit(solution)/shard_map/all_to_all | solution.py:88
  450.0 8.4 %convert_reduce_fusion = f32[128,1536]{1,0:T(8,128)S(1)} fusion(bf16[32,128,1536]{2,1,0:T(8,128)(2,1)} %bitcast.32, bf16[32,128,128]{2,1,0:T(8,128)(2,1)} %all-to-all-done.1), kind=kOutput, calls=%fused_computation.2 | convolution fusion | flops 1629290496 | bytes 14417920 | tf_op jit(solution)/shard_map/rgk,gkd->grd/dot_general | solution.py:91
  464.6 2.9 fusion.81
  (89 shorter events, 28.5 us)
Async XLA Ops:
  6.5 314.6 %copy-start = (bf16[768,1536]{1,0:T(8,128)(2,1)S(1)}, bf16[768,1536]{1,0:T(8,128)(2,1)}, u32[]{:S(2)}) copy-start(bf16[768,1536]{1,0:T(8,128)(2,1)} %param.23) | copy-start | bytes 7077892
  13.6 10.4 %copy-start.8 = (bf16[1,2,256,384]{3,2,1,0:T(8,128)(2,1)S(1)}, bf16[1,2,256,384]{3,2,1,0:T(8,128)(2,1)}, u32[]{:S(2)}) copy-start(bf16[1,2,256,384]{3,2,1,0:T(8,128)(2,1)} %param.15) | copy-start | bytes 1179652
  13.6 301.5 %all-to-all-start = ((bf16[32,128,1536]{2,1,0:T(8,128)(2,1)}), bf16[32,128,1536]{2,1,0:T(8,128)(2,1)}, u32[]{:S(2)}, u32[]{:S(2)}) async-start(bf16[32,128,1536]{2,1,0:T(8,128)(2,1)} %broadcast_in_dim.20), calls=%async_computation | async-start | bytes 25165824 | tf_op jit(solution)/shard_map/all_to_all | solution.py:152
  24.0 378.4 %all-gather.2.cloned.1.call-start = ((), (), s32[]{:S(2)}) async-start(), calls=%async_computation.2 | async-start | bytes 12976128 | tf_op jit(solution)/shard_map/all_gather | solution.py:84
  24.0 222.7 %collective-permute-start = (bf16[2,256,384]{2,1,0:T(8,128)(2,1)S(1)}, bf16[2,256,384]{2,1,0:T(8,128)(2,1)S(1)}, u32[]{:S(2)}, u32[]{:S(2)}) collective-permute-start(bf16[2,256,384]{2,1,0:T(8,128)(2,1)S(1)} %bitcast.156), channel_id=1, source_target_pairs={{0,128},{32,160},{64,192},{96,224},{128,0},{160,32},{192,64},{224,... | collective-permute-start | bytes 1179656 | tf_op jit(solution)/shard_map/ppermute | solution.py:109
  26.9 214.4 %collective-permute-start.1 = (s32[1]{0:T(128)}, s32[1]{0:T(128)}, u32[]{:S(2)}, u32[]{:S(2)}) collective-permute-start(s32[1]{0:T(128)} %param.17), channel_id=1, source_target_pairs={{0,32},{32,0},{64,96},{96,64},{128,160},{160,128},{192,224},{224,1... | collective-permute-start | bytes 20 | tf_op jit(solution)/shard_map/ppermute | solution.py:109
  31.8 5.0 %copy-start.2 = (bf16[1,128,1536]{2,1,0:T(8,128)(2,1)S(1)}, bf16[1,128,1536]{2,1,0:T(8,128)(2,1)}, u32[]{:S(2)}) copy-start(bf16[1,128,1536]{2,1,0:T(8,128)(2,1)} %param.14) | copy-start | bytes 1179652
  31.8 5.2 %copy-start.17 = (f32[1536]{0:T(1024)S(1)}, f32[1536]{0:T(1024)}, u32[]{:S(2)}) copy-start(f32[1536]{0:T(1024)} %param.19) | copy-start | bytes 18436
  242.0 2.8 collective-permute-start.2
  247.8 17.5 %collective-permute-start.3 = (bf16[2,2,256,384]{3,2,1,0:T(8,128)(2,1)}, bf16[2,2,256,384]{3,2,1,0:T(8,128)(2,1)}, u32[]{:S(2)}, u32[]{:S(2)}) collective-permute-start(bf16[2,2,256,384]{3,2,1,0:T(8,128)(2,1)} %pad_maximum_fusion), channel_id=1, source_target_pairs={{0,64},{32,96},{64,0},{96,32},{128,192},{160,224},{192,128},{224,1... | collective-permute-start | bytes 2359304 | tf_op jit(solution)/shard_map/ppermute | solution.py:109
  252.3 4.2 copy-start.7
  267.1 12.1 %collective-permute-start.4 = (bf16[2,256,384]{2,1,0:T(8,128)(2,1)}, bf16[2,256,384]{2,1,0:T(8,128)(2,1)}, u32[]{:S(2)}, u32[]{:S(2)}) collective-permute-start(bf16[2,256,384]{2,1,0:T(8,128)(2,1)} %fusion.28), channel_id=1, source_target_pairs={{0,32},{32,0},{64,96},{96,64},{128,160},{160,128},{192,224},{224,1... | collective-permute-start | bytes 1179656 | tf_op jit(solution)/shard_map/ppermute | solution.py:109
  281.1 35.4 %copy-start.18 = (bf16[128,4,48]{0,2,1:T(8,128)(2,1)S(1)}, bf16[128,4,48]{0,2,1:T(8,128)(2,1)}, u32[]{:S(2)}) copy-start(bf16[128,4,48]{0,2,1:T(8,128)(2,1)} %get-tuple-element.21) | copy-start | bytes 147460
  281.1 35.4 %copy-start.19 = (bf16[128,4,48]{0,2,1:T(8,128)(2,1)S(1)}, bf16[128,4,48]{0,2,1:T(8,128)(2,1)}, u32[]{:S(2)}) copy-start(bf16[128,4,48]{0,2,1:T(8,128)(2,1)} %get-tuple-element.22) | copy-start | bytes 147460
  316.4 3.0 copy-start.15
  316.5 2.9 copy-start.13
  316.5 2.9 copy-start.16
  321.7 80.7 %copy-start.12 = (bf16[1536,128]{1,0:T(8,128)(2,1)S(1)}, bf16[1536,128]{1,0:T(8,128)(2,1)}, u32[]{:S(2)}) copy-start(bf16[1536,128]{1,0:T(8,128)(2,1)} %param.25) | copy-start | bytes 1179652
  323.5 86.8 %copy-start.22 = (bf16[1536,128]{1,0:T(8,128)(2,1)S(1)}, bf16[1536,128]{1,0:T(8,128)(2,1)}, u32[]{:S(2)}) copy-start(bf16[1536,128]{1,0:T(8,128)(2,1)} %param.26) | copy-start | bytes 1179652
  402.4 8.2 %copy-start.1 = (bf16[4096,1536]{1,0:T(8,128)(2,1)S(1)}, bf16[4096,1536]{1,0:T(8,128)(2,1)}, u32[]{:S(2)}) copy-start(bf16[4096,1536]{1,0:T(8,128)(2,1)} %all-gather.2.cloned.1.call-done) | copy-start | bytes 37748740
  415.2 6.9 %copy-start.23 = (s32[1,128]{1,0:T(1,128)S(1)}, s32[1,128]{1,0:T(1,128)}, u32[]{:S(2)}) copy-start(s32[1,128]{1,0:T(1,128)} %param.18) | copy-start | bytes 1540
  415.2 34.8 %all-to-all-start.1 = ((bf16[32,128,128]{2,1,0:T(8,128)(2,1)}), bf16[32,128,128]{2,1,0:T(8,128)(2,1)}, u32[]{:S(2)}, u32[]{:S(2)}) async-start(bf16[32,128,128]{2,1,0:T(8,128)(2,1)} %bitcast.158), calls=%async_computation.1 | async-start | bytes 2097152 | tf_op jit(solution)/shard_map/all_to_all | solution.py:88
  449.9 8.4 %copy-start.5 = (f32[128,1536]{1,0:T(8,128)S(1)}, f32[128,1536]{1,0:T(8,128)}, u32[]{:S(2)}) copy-start(f32[128,1536]{1,0:T(8,128)} %copy-done.4) | copy-start | bytes 2359300
  464.5 2.9 copy-start.14
  (8 other events, 12.2 us)
Sparse Core Ops, SparseCore 0:
  323.7 78.6 all-gather.1
where the time goes:
time: 478 us; the launch traced here: 477 us
  waiting for transfers between devices  355 us (74%)
  matrix products  40.9 us (9%)
  starting transfers between devices  28 us (6%)
  local copies, waits for them, and re-layouts  20.8 us (4%)
  between operations  17.6 us (4%)
  other arithmetic  14.9 us (3%)
    ppermute x5, waiting for transfers between devices, swap(): lax.ppermute(values, 'req', perm=[(i, i ^ mask) for i in range(count)])  214 us
    all_gather x1, waiting for transfers between devices, run_ffn(): part_rows = lax.all_gather(normed_rows, 'blk', axis=0, tiled=True)  78.8 us
    all_to_all x1, waiting for transfers between devices, local(): lax.all_to_all(copies, 'blk', 0, 0, tiled=True).reshape(-1, w_down.shape[1])  34 us
    all_to_all x1, waiting for transfers between devices, run_ffn(): hidden_own = lax.all_to_all(hidden_all, 'blk', 0, 1, tiled=True)  27.9 us
    ppermute x5, starting transfers between devices, swap(): lax.ppermute(values, 'req', perm=[(i, i ^ mask) for i in range(count)])  10.7 us
    all_to_all x1, starting transfers between devices, local(): lax.all_to_all(copies, 'blk', 0, 0, tiled=True).reshape(-1, w_down.shape[1])  10.4 us
    unnamed x50, local copies, waits for them, and re-layouts  9.99 us
  transfers between devices with their start and end apart: 8, of which 7 were waited for; matrix products, arithmetic and copies ran while one was open for 6% of the time, Pallas kernels for 0%

commit v1 on v0

--- a/solution.py
+++ b/solution.py
@@ -85,7 +85,10 @@
     gate_vals = jnp.dot(part_rows, w_gate, preferred_element_type=jnp.float32)
     up_vals = jnp.dot(part_rows, w_up, preferred_element_type=jnp.float32)
     hidden_all = (jax.nn.silu(gate_vals) * up_vals).astype(jnp.bfloat16)
-    hidden_own = lax.all_to_all(hidden_all, "blk", 0, 1, tiled=True)
+    n_dev = lax.axis_size("blk")
+    blocks = jnp.stack(jnp.split(hidden_all, n_dev, axis=0), axis=0)
+    blocks = lax.all_to_all(blocks, "blk", split_axis=0, concat_axis=0)
+    hidden_own = jnp.concatenate(blocks, axis=1)
     groups = w_down.shape[0]
     group_count = down_all.shape[0] // groups
     terms = jnp.einsum(

time: 478 us -> 494 us (1.033)
  local copies, waits for them, and re-layouts: 20.8 us -> 40.4 us
    unnamed x50 -> x85, local copies, waits for them, and re-layouts: 9.99 us -> 29 us
where the time goes in v1:
time: 494 us
  waiting for transfers between devices  355 us (72%)
  local copies, waits for them, and re-layouts  40.4 us (8%)
  matrix products  38.9 us (8%)
  starting transfers between devices  27.8 us (6%)
  between operations  17.5 us (4%)
  other arithmetic  13.5 us (3%)
    ppermute x5, waiting for transfers between devices, swap(): lax.ppermute(values, 'req', perm=[(i, i ^ mask) for i in range(count)])  214 us
    all_gather x1, waiting for transfers between devices, run_ffn(): part_rows = lax.all_gather(normed_rows, 'blk', axis=0, tiled=True)  78.8 us
    all_to_all x1, waiting for transfers between devices, local(): lax.all_to_all(copies, 'blk', 0, 0, tiled=True).reshape(-1, w_down.shape[1])  34.1 us
    unnamed x85, local copies, waits for them, and re-layouts  29 us
    all_to_all x1, waiting for transfers between devices, run_ffn(): blocks = lax.all_to_all(blocks, 'blk', split_axis=0, concat_axis=0)  27.9 us
    ppermute x5, starting transfers between devices, swap(): lax.ppermute(values, 'req', perm=[(i, i ^ mask) for i in range(count)])  10.7 us
    all_to_all x1, starting transfers between devices, local(): lax.all_to_all(copies, 'blk', 0, 0, tiled=True).reshape(-1, w_down.shape[1])  10.4 us
  transfers between devices with their start and end apart: 8, of which 7 were waited for; matrix products, arithmetic and copies ran while one was open for 6% of the time, Pallas kernels for 0%

profile of v1, /device:TPU:1, one launch (start us, length us, event | category | flops | bytes accessed | tf_op | source)
XLA Modules:
  0.0 493.5 jit_solution(16154002641867106493)
XLA Ops:
  6.5 7.1 %broadcast_in_dim.20 = bf16[32,128,1536]{2,1,0:T(8,128)(2,1)} broadcast(bf16[128,1536]{1,0:T(8,128)(2,1)} %param.27), dimensions={1,2} | broadcast | bytes 12976128 | tf_op jit(solution)/shard_map/broadcast_in_dim | solution.py:154
  13.6 10.4 %all-to-all-start = ((bf16[32,128,1536]{2,1,0:T(8,128)(2,1)}), bf16[32,128,1536]{2,1,0:T(8,128)(2,1)}, u32[]{:S(2)}, u32[]{:S(2)}) async-start(bf16[32,128,1536]{2,1,0:T(8,128)(2,1)} %broadcast_in_dim.20), calls=%async_computation | async-start | bytes 25165824 | tf_op jit(solution)/shard_map/all_to_all | solution.py:155
  24.1 2.8 collective-permute-start
  26.9 4.2 collective-permute-start.1
  31.8 4.3 copy.29
  37.0 3.3 fusion.55
  40.8 200.5 %collective-permute-done.1 = s32[1]{0:T(128)} collective-permute-done((s32[1]{0:T(128)}, s32[1]{0:T(128)}, u32[]{:S(2)}, u32[]{:S(2)}) %collective-permute-start.1) | collective-permute-done | bytes 36 | tf_op jit(solution)/shard_map/ppermute | solution.py:112
  249.7 2.5 copy.28
  252.2 1.9 subtract_convert_fusion.1
  254.1 2.3 convolution_convert_fusion.4
  258.7 6.4 %collective-permute-done.3 = bf16[2,2,256,384]{3,2,1,0:T(8,128)(2,1)} collective-permute-done((bf16[2,2,256,384]{3,2,1,0:T(8,128)(2,1)}, bf16[2,2,256,384]{3,2,1,0:T(8,128)(2,1)}, u32[]{:S(2)}, u32[]{:S(2)}) %collective-permute-start.3) | collective-permute-done | bytes 786464 | tf_op jit(solution)/shard_map/ppermute | solution.py:112
  265.2 1.8 fusion.28
  273.1 6.0 %collective-permute-done.4 = bf16[2,256,384]{2,1,0:T(8,128)(2,1)} collective-permute-done((bf16[2,256,384]{2,1,0:T(8,128)(2,1)}, bf16[2,256,384]{2,1,0:T(8,128)(2,1)}, u32[]{:S(2)}, u32[]{:S(2)}) %collective-permute-start.4) | collective-permute-done | bytes 393248 | tf_op jit(solution)/shard_map/ppermute | solution.py:112
  279.1 1.9 fusion.24
  281.0 34.1 %all-to-all-done = bf16[32,128,1536]{2,1,0:T(8,128)(2,1)} async-done(((bf16[32,128,1536]{2,1,0:T(8,128)(2,1)}), bf16[32,128,1536]{2,1,0:T(8,128)(2,1)}, u32[]{:S(2)}, u32[]{:S(2)}) %all-to-all-start) | async-done | bytes 12582944 | tf_op jit(solution)/shard_map/all_to_all | solution.py:155
  316.6 2.8 fusion.78
  322.8 78.8 %all-gather.2.cloned.1.call-done = bf16[4096,1536]{1,0:T(8,128)(2,1)} async-done(((bf16[128,1536]{1,0:T(8,128)(2,1)}), bf16[4096,1536]{1,0:T(8,128)(2,1)}) %all-gather.2.cloned.1.call-update) | async-done | bytes 12582928 | tf_op jit(solution)/shard_map/all_gather | solution.py:84
  401.6 8.0 %fusion.84 = f32[4096,128]{1,0:T(8,128)S(1)} fusion(bf16[4096,1536]{1,0:T(8,128)(2,1)} %all-gather.2.cloned.1.call-done, bf16[1536,128]{1,0:T(8,128)(2,1)} %param.25), kind=kOutput, calls=%fused_computation.169 | convolution fusion | flops 1610612736 | bytes 15073280 | tf_op jit(solution)/shard_map/dot_general | solution.py:85
  409.9 3.7 fusion.2
  433.2 6.7 %all-to-all-start.1 = ((bf16[32,128,128]{2,1,0:T(8,128)(2,1)}), bf16[32,128,128]{2,1,0:T(8,128)(2,1)}, u32[]{:S(2)}, u32[]{:S(2)}) async-start(bf16[32,128,128]{2,1,0:T(8,128)(2,1)} %constant_dynamic-update-slice_fusion), calls=%async_computation.1 | async-start | bytes 2097152 | tf_op jit(solution)/shard_map/all_to_all | solution.py:90
  440.0 27.9 %all-to-all-done.1 = bf16[32,128,128]{2,1,0:T(8,128)(2,1)} async-done(((bf16[32,128,128]{2,1,0:T(8,128)(2,1)}), bf16[32,128,128]{2,1,0:T(8,128)(2,1)}, u32[]{:S(2)}, u32[]{:S(2)}) %all-to-all-start.1) | async-done | bytes 1048608 | tf_op jit(solution)/shard_map/all_to_all | solution.py:90
  467.9 8.3 %convert_reduce_fusion = f32[128,1536]{1,0:T(8,128)S(1)} fusion(bf16[32,128,1536]{2,1,0:T(8,128)(2,1)} %bitcast.63, bf16[32,128,128]{2,1,0:T(8,128)(2,1)} %all-to-all-done.1), kind=kOutput, calls=%fused_computation.2 | convolution fusion | flops 1629290496 | bytes 14417920 | tf_op jit(solution)/shard_map/rgk,gkd->grd/dot_general | solution.py:94
  481.7 1.8 fusion.81
  483.5 1.8 convolution_convert_fusion.1
  (125 shorter events, 46.6 us)
Async XLA Ops:
  6.5 314.6 %copy-start = (bf16[768,1536]{1,0:T(8,128)(2,1)S(1)}, bf16[768,1536]{1,0:T(8,128)(2,1)}, u32[]{:S(2)}) copy-start(bf16[768,1536]{1,0:T(8,128)(2,1)} %param.23) | copy-start | bytes 7077892
  13.6 10.4 %copy-start.8 = (bf16[1,2,256,384]{3,2,1,0:T(8,128)(2,1)S(1)}, bf16[1,2,256,384]{3,2,1,0:T(8,128)(2,1)}, u32[]{:S(2)}) copy-start(bf16[1,2,256,384]{3,2,1,0:T(8,128)(2,1)} %param.15) | copy-start | bytes 1179652
  13.6 301.5 %all-to-all-start = ((bf16[32,128,1536]{2,1,0:T(8,128)(2,1)}), bf16[32,128,1536]{2,1,0:T(8,128)(2,1)}, u32[]{:S(2)}, u32[]{:S(2)}) async-start(bf16[32,128,1536]{2,1,0:T(8,128)(2,1)} %broadcast_in_dim.20), calls=%async_computation | async-start | bytes 25165824 | tf_op jit(solution)/shard_map/all_to_all | solution.py:155
  24.0 377.6 %all-gather.2.cloned.1.call-start = ((), (), s32[]{:S(2)}) async-start(), calls=%async_computation.2 | async-start | bytes 12976128 | tf_op jit(solution)/shard_map/all_gather | solution.py:84
  24.1 222.6 %collective-permute-start = (bf16[2,256,384]{2,1,0:T(8,128)(2,1)S(1)}, bf16[2,256,384]{2,1,0:T(8,128)(2,1)S(1)}, u32[]{:S(2)}, u32[]{:S(2)}) collective-permute-start(bf16[2,256,384]{2,1,0:T(8,128)(2,1)S(1)} %bitcast.283), channel_id=1, source_target_pairs={{0,128},{32,160},{64,192},{96,224},{128,0},{160,32},{192,64},{224,... | collective-permute-start | bytes 1179656 | tf_op jit(solution)/shard_map/ppermute | solution.py:112
  26.9 214.4 %collective-permute-start.1 = (s32[1]{0:T(128)}, s32[1]{0:T(128)}, u32[]{:S(2)}, u32[]{:S(2)}) collective-permute-start(s32[1]{0:T(128)} %param.17), channel_id=1, source_target_pairs={{0,32},{32,0},{64,96},{96,64},{128,160},{160,128},{192,224},{224,1... | collective-permute-start | bytes 20 | tf_op jit(solution)/shard_map/ppermute | solution.py:112
  31.8 5.0 %copy-start.2 = (bf16[1,128,1536]{2,1,0:T(8,128)(2,1)S(1)}, bf16[1,128,1536]{2,1,0:T(8,128)(2,1)}, u32[]{:S(2)}) copy-start(bf16[1,128,1536]{2,1,0:T(8,128)(2,1)} %param.14) | copy-start | bytes 1179652
  31.8 5.2 %copy-start.17 = (f32[1536]{0:T(1024)S(1)}, f32[1536]{0:T(1024)}, u32[]{:S(2)}) copy-start(f32[1536]{0:T(1024)} %param.19) | copy-start | bytes 18436
  241.9 2.8 collective-permute-start.2
  246.6 2.3 copy-start.21
  247.7 17.5 %collective-permute-start.3 = (bf16[2,2,256,384]{3,2,1,0:T(8,128)(2,1)}, bf16[2,2,256,384]{3,2,1,0:T(8,128)(2,1)}, u32[]{:S(2)}, u32[]{:S(2)}) collective-permute-start(bf16[2,2,256,384]{3,2,1,0:T(8,128)(2,1)} %pad_maximum_fusion), channel_id=1, source_target_pairs={{0,64},{32,96},{64,0},{96,32},{128,192},{160,224},{192,128},{224,1... | collective-permute-start | bytes 2359304 | tf_op jit(solution)/shard_map/ppermute | solution.py:112
  252.2 4.2 copy-start.7
  267.0 12.1 %collective-permute-start.4 = (bf16[2,256,384]{2,1,0:T(8,128)(2,1)}, bf16[2,256,384]{2,1,0:T(8,128)(2,1)}, u32[]{:S(2)}, u32[]{:S(2)}) collective-permute-start(bf16[2,256,384]{2,1,0:T(8,128)(2,1)} %fusion.28), channel_id=1, source_target_pairs={{0,32},{32,0},{64,96},{96,64},{128,160},{160,128},{192,224},{224,1... | collective-permute-start | bytes 1179656 | tf_op jit(solution)/shard_map/ppermute | solution.py:112
  269.8 46.8 %copy-start.24 = (pred[384]{0:T(512)(128)(4,1)}, pred[384]{0:T(512)(128)(4,1)S(1)}, u32[]{:S(2)}) copy-start(pred[384]{0:T(512)(128)(4,1)S(1)} %concatenate.51) | copy-start | bytes 1156
  281.0 35.6 %copy-start.18 = (bf16[128,4,48]{0,2,1:T(8,128)(2,1)S(1)}, bf16[128,4,48]{0,2,1:T(8,128)(2,1)}, u32[]{:S(2)}) copy-start(bf16[128,4,48]{0,2,1:T(8,128)(2,1)} %get-tuple-element.21) | copy-start | bytes 147460
  281.0 35.6 %copy-start.19 = (bf16[128,4,48]{0,2,1:T(8,128)(2,1)S(1)}, bf16[128,4,48]{0,2,1:T(8,128)(2,1)}, u32[]{:S(2)}) copy-start(bf16[128,4,48]{0,2,1:T(8,128)(2,1)} %get-tuple-element.22) | copy-start | bytes 147460
  316.4 3.0 copy-start.14
  316.5 2.9 copy-start.12
  316.6 2.9 copy-start.16
  401.6 8.3 %copy-start.1 = (bf16[4096,1536]{1,0:T(8,128)(2,1)S(1)}, bf16[4096,1536]{1,0:T(8,128)(2,1)}, u32[]{:S(2)}) copy-start(bf16[4096,1536]{1,0:T(8,128)(2,1)} %all-gather.2.cloned.1.call-done) | copy-start | bytes 37748740
  401.6 8.3 %copy-start.22 = (bf16[1536,128]{1,0:T(8,128)(2,1)S(1)}, bf16[1536,128]{1,0:T(8,128)(2,1)}, u32[]{:S(2)}) copy-start(bf16[1536,128]{1,0:T(8,128)(2,1)} %param.26) | copy-start | bytes 1179652
  423.4 16.6 %copy-start.23 = (s32[1,128]{1,0:T(1,128)S(1)}, s32[1,128]{1,0:T(1,128)}, u32[]{:S(2)}) copy-start(s32[1,128]{1,0:T(1,128)} %param.18) | copy-start | bytes 1540
  433.2 34.7 %all-to-all-start.1 = ((bf16[32,128,128]{2,1,0:T(8,128)(2,1)}), bf16[32,128,128]{2,1,0:T(8,128)(2,1)}, u32[]{:S(2)}, u32[]{:S(2)}) async-start(bf16[32,128,128]{2,1,0:T(8,128)(2,1)} %constant_dynamic-update-slice_fusion), calls=%async_computation.1 | async-start | bytes 2097152 | tf_op jit(solution)/shard_map/all_to_all | solution.py:90
  476.2 2.0 copy-start.3
  (10 other events, 12.9 us)
Sparse Core Ops, SparseCore 0:
  322.9 78.6 all-gather.1
